TPU v7x, 512 devices: a whole 4x8x8 slice. The times are simulated.
512 devices in a mesh: frame: 8 (over y), space: 32 (over z, x), dp: 2 (over core).
Axes of the slice: x: 4, y: 8, z: 8, core: 2. Of those that a mesh axis runs over, the one named last changes fastest.
Arguments:
- frames_in: bfloat16 [16, 4096, 768], P(('dp', 'frame'), 'space'), parts along dimension 0, may hold values from -6 to 6
- cotangent: bfloat16 [16, 4096, 768], P(('dp', 'frame'), 'space'), parts along dimension 0, may hold values from -6 to 6
- w_qkv_space: bfloat16 [768, 2304], P('space'), may hold values from -0.21875 to 0.21875
- w_out_space: bfloat16 [768, 768], P('space'), may hold values from -0.875 to 0.875
- w_qkv_time: bfloat16 [768, 2304], P('space'), may hold values from -0.21875 to 0.21875
- w_out_time: bfloat16 [768, 768], P('space'), may hold values from -0.21875 to 0.21875
- neighbours: int32 [32, 4], replicated, may hold values from 0 to 31, as said below
Outputs:
- frames_out: bfloat16 [16, 4096, 768], P(('dp', 'frame'), 'space'), parts along dimension 0
- grad_frames: bfloat16 [16, 4096, 768], P(('dp', 'frame'), 'space'), parts along dimension 0
There are 2 independent parts, one for each index of `dp`. A program takes and returns all parts, laid end to end along the dimension named above; an argument that names none is the same for every part. Nothing has to cross between parts.
Inputs may be any that keep to these rules, and one draw needn't show every extreme that they name: `neighbours`: row b lists block b first; every entry c satisfies |c - b| <= 1; entries may repeat, and a repeated entry counts once.
All inputs are finite; a program needn't handle non-finite values.
Results may differ from a plain program's by a relative error of at most 0.023.
Values may be sent and summed in bfloat16 or wider, within the bound.
No kernel may reach another device: no remote copies, remote signals or barrier semaphores. Data moves between devices by JAX's collectives and lax.ppermute only.
A program may use at most 64 MiB of HBM per device.

v0:
```python
import jax
import jax.numpy as jnp
from jax import lax
from jax.sharding import PartitionSpec as P

HEADS = 12
HD = 64
BLOCK = 128
EPS = 1e-06


def padded(cells, sides, width):
    for axis, dim in sides:
        count = lax.axis_size(axis)
        ends = count - 1
        head = lax.slice_in_dim(cells, 0, width, axis=dim)
        tail = lax.slice_in_dim(cells, cells.shape[dim] - width, cells.shape[dim], axis=dim)
        cells = jnp.concatenate(
            [
                lax.ppermute(tail, axis, [(i, (i + 1) % count) for i in range(ends)]),
                cells,
                lax.ppermute(head, axis, [((i + 1) % count, i) for i in range(ends)]),
            ],
            axis=dim,
        )
    return cells


def rms_norm(row_data):
    values = row_data.astype(jnp.float32)
    factor = lax.rsqrt(jnp.mean(values * values, axis=-1, keepdims=True) + EPS)
    return (values * factor).astype(jnp.bfloat16)


def rms_back(row_data, upstream):
    values = row_data.astype(jnp.float32)
    factor = lax.rsqrt(jnp.mean(values * values, axis=-1, keepdims=True) + EPS)
    inner_mean = jnp.mean(values * upstream, axis=-1, keepdims=True)
    return factor * upstream - values * factor**3 * inner_mean


def block_mask(neighbour_rows, first_id):
    block_count = neighbour_rows.shape[0]
    candidate = first_id + jnp.arange(3 * block_count, dtype=jnp.int32)
    matches = jnp.any(neighbour_rows[:, :, None] == candidate[None, None, :], axis=1)
    return jnp.repeat(jnp.repeat(matches, BLOCK, axis=0), BLOCK, axis=1)


def space_attend(queries, key_rows, value_rows, allowed):
    score_scale = HD ** (-0.5)
    query_count = queries.shape[0]
    key_count = key_rows.shape[0]
    output_list = []
    total_list = []
    for head_pair in range(HEADS // 2):
        start_col = head_pair * 2 * HD
        stop_col = start_col + 2 * HD
        query_part = queries[:, start_col:stop_col].reshape(query_count, 2, HD)
        key_part = key_rows[:, start_col:stop_col].reshape(key_count, 2, HD)
        value_part = value_rows[:, start_col:stop_col].reshape(key_count, 2, HD)
        scores = (
            jnp.einsum("sgh,tgh->gst", query_part, key_part, preferred_element_type=jnp.float32)
            * score_scale
        )
        exponent = jnp.where(allowed[None], jnp.exp(scores), 0.0)
        totals = jnp.sum(exponent, axis=-1)
        probability = (exponent / totals[:, :, None]).astype(jnp.bfloat16)
        combined = jnp.einsum(
            "gst,tgh->sgh", probability, value_part, preferred_element_type=jnp.float32
        )
        output_list.append(combined.astype(jnp.bfloat16).reshape(query_count, 2 * HD))
        total_list.append(totals)
    return (jnp.concatenate(output_list, axis=1), jnp.concatenate(total_list, axis=0))


def space_back(queries, key_rows, value_rows, allowed, totals, attended, grad_attended):
    score_scale = HD ** (-0.5)
    query_count = queries.shape[0]
    key_count = key_rows.shape[0]
    query_list = []
    key_list = []
    value_list = []
    for head_pair in range(HEADS // 2):
        start_col = head_pair * 2 * HD
        stop_col = start_col + 2 * HD
        query_part = queries[:, start_col:stop_col].reshape(query_count, 2, HD)
        key_part = key_rows[:, start_col:stop_col].reshape(key_count, 2, HD)
        value_part = value_rows[:, start_col:stop_col].reshape(key_count, 2, HD)
        out_part = attended[:, start_col:stop_col].reshape(query_count, 2, HD)
        grad_part = grad_attended[:, start_col:stop_col].reshape(query_count, 2, HD)
        scores = (
            jnp.einsum("sgh,tgh->gst", query_part, key_part, preferred_element_type=jnp.float32)
            * score_scale
        )
        exponent = jnp.where(allowed[None], jnp.exp(scores), 0.0)
        weight = exponent / totals[2 * head_pair : 2 * head_pair + 2, :, None]
        probability = weight.astype(jnp.bfloat16)
        prob_grad = jnp.einsum(
            "sgh,tgh->gst", grad_part, value_part, preferred_element_type=jnp.float32
        )
        row_delta = jnp.einsum(
            "sgh,sgh->gs", grad_part, out_part, preferred_element_type=jnp.float32
        )
        score_grad = (weight * (prob_grad - row_delta[:, :, None])).astype(jnp.bfloat16)
        query_grad = (
            jnp.einsum("gst,tgh->sgh", score_grad, key_part, preferred_element_type=jnp.float32)
            * score_scale
        )
        key_grad = (
            jnp.einsum("gst,sgh->tgh", score_grad, query_part, preferred_element_type=jnp.float32)
            * score_scale
        )
        value_grad = jnp.einsum(
            "gst,sgh->tgh", probability, grad_part, preferred_element_type=jnp.float32
        )
        query_list.append(query_grad.astype(jnp.bfloat16).reshape(query_count, 2 * HD))
        key_list.append(key_grad.reshape(key_count, 2 * HD))
        value_list.append(value_grad.reshape(key_count, 2 * HD))
    return (
        jnp.concatenate(query_list, axis=1),
        jnp.concatenate(key_list, axis=1),
        jnp.concatenate(value_list, axis=1),
    )


def time_attend(queries, key_rows, value_rows):
    frame_count, position_count, feature_count = queries.shape
    split_shape = (frame_count, position_count, HEADS, HD)
    score_scale = HD ** (-0.5)
    scores = (
        jnp.einsum(
            "fphd,gphd->phfg",
            queries.reshape(split_shape),
            key_rows.reshape(split_shape),
            preferred_element_type=jnp.float32,
        )
        * score_scale
    )
    causal = jnp.arange(frame_count)[:, None] >= jnp.arange(frame_count)[None, :]
    exponent = jnp.where(causal, jnp.exp(scores), 0.0)
    totals = jnp.sum(exponent, axis=-1)
    probability = (exponent / totals[..., None]).astype(jnp.bfloat16)
    combined = jnp.einsum(
        "phfg,gphd->fphd",
        probability,
        value_rows.reshape(split_shape),
        preferred_element_type=jnp.float32,
    )
    return (
        combined.astype(jnp.bfloat16).reshape(frame_count, position_count, feature_count),
        totals,
    )


def time_back(queries, key_rows, value_rows, attended, grad_attended, totals):
    frame_count, position_count, feature_count = queries.shape
    split_shape = (frame_count, position_count, HEADS, HD)
    score_scale = HD ** (-0.5)
    query_four = queries.reshape(split_shape)
    key_four = key_rows.reshape(split_shape)
    value_four = value_rows.reshape(split_shape)
    out_four = attended.reshape(split_shape)
    grad_four = grad_attended.reshape(split_shape)
    scores = (
        jnp.einsum("fphd,gphd->phfg", query_four, key_four, preferred_element_type=jnp.float32)
        * score_scale
    )
    causal = jnp.arange(frame_count)[:, None] >= jnp.arange(frame_count)[None, :]
    exponent = jnp.where(causal, jnp.exp(scores), 0.0)
    weight = exponent / totals[..., None]
    probability = weight.astype(jnp.bfloat16)
    prob_grad = jnp.einsum(
        "fphd,gphd->phfg", grad_four, value_four, preferred_element_type=jnp.float32
    )
    row_delta = jnp.einsum(
        "fphd,fphd->phf", grad_four, out_four, preferred_element_type=jnp.float32
    )
    score_grad = (weight * (prob_grad - row_delta[..., None])).astype(jnp.bfloat16)
    query_grad = (
        jnp.einsum("phfg,gphd->fphd", score_grad, key_four, preferred_element_type=jnp.float32)
        * score_scale
    )
    key_grad = (
        jnp.einsum("phfg,fphd->gphd", score_grad, query_four, preferred_element_type=jnp.float32)
        * score_scale
    )
    value_grad = jnp.einsum(
        "phfg,fphd->gphd", probability, grad_four, preferred_element_type=jnp.float32
    )
    pieces = [
        gradient.astype(jnp.bfloat16).reshape(frame_count, position_count, feature_count)
        for gradient in (query_grad, key_grad, value_grad)
    ]
    return jnp.concatenate(pieces, axis=-1)


def to_frames(local_rows):
    return lax.all_to_all(local_rows[None], "frame", split_axis=1, concat_axis=0, tiled=True)


def to_space(frame_rows):
    return lax.all_to_all(frame_rows, "frame", split_axis=0, concat_axis=1, tiled=True)[0]


def rim(first_part, second_part, width):
    return (padded(first_part, (("space", 0),), width), padded(second_part, (("space", 0),), width))


def local(frames_in, cotangent, w_qkv_space, w_out_space, w_qkv_time, w_out_time, neighbours):
    local_in = frames_in[0]
    grad_out = cotangent[0]
    shard, feature_count = local_in.shape
    full_qkv_space, full_out_space, full_qkv_time, full_out_time = (
        lax.all_gather(w_qkv_space, "space", axis=0, tiled=True),
        lax.all_gather(w_out_space, "space", axis=0, tiled=True),
        lax.all_gather(w_qkv_time, "space", axis=0, tiled=True),
        lax.all_gather(w_out_time, "space", axis=0, tiled=True),
    )
    block_count = shard // BLOCK
    space_index = lax.axis_index("space")
    lists_here = lax.dynamic_slice_in_dim(neighbours, space_index * block_count, block_count, 0)
    allowed = block_mask(lists_here, (space_index - 1) * block_count)
    normed_space = rms_norm(local_in)
    projected = jnp.dot(normed_space, full_qkv_space, preferred_element_type=jnp.float32).astype(
        jnp.bfloat16
    )
    queries = projected[:, :feature_count]
    key_window, value_window = rim(
        projected[:, feature_count : 2 * feature_count], projected[:, 2 * feature_count :], shard
    )
    attended, totals = space_attend(queries, key_window, value_window, allowed)
    update = jnp.dot(attended, full_out_space, preferred_element_type=jnp.float32)
    stream = (local_in.astype(jnp.float32) + update).astype(jnp.bfloat16)
    normed_time = rms_norm(stream)
    projected_time = jnp.dot(normed_time, full_qkv_time, preferred_element_type=jnp.float32).astype(
        jnp.bfloat16
    )
    time_rows = to_frames(projected_time)
    query_time = time_rows[..., :feature_count]
    key_time = time_rows[..., feature_count : 2 * feature_count]
    value_time = time_rows[..., 2 * feature_count :]
    attended_time, totals_time = time_attend(query_time, key_time, value_time)
    attended_back = to_space(attended_time)
    update_time = jnp.dot(attended_back, full_out_time, preferred_element_type=jnp.float32)
    frames_out = (stream.astype(jnp.float32) + update_time).astype(jnp.bfloat16)
    grad_att_time = jnp.dot(grad_out, full_out_time.T, preferred_element_type=jnp.float32).astype(
        jnp.bfloat16
    )
    grad_time_rows = to_frames(grad_att_time)
    gradients = time_back(
        query_time, key_time, value_time, attended_time, grad_time_rows, totals_time
    )
    grad_project_time = to_space(gradients)
    grad_normed_time = jnp.dot(
        grad_project_time, full_qkv_time.T, preferred_element_type=jnp.float32
    )
    grad_stream = (grad_out.astype(jnp.float32) + rms_back(stream, grad_normed_time)).astype(
        jnp.bfloat16
    )
    grad_attended = jnp.dot(
        grad_stream, full_out_space.T, preferred_element_type=jnp.float32
    ).astype(jnp.bfloat16)
    grad_query, key_partial, value_partial = space_back(
        queries, key_window, value_window, allowed, totals, attended, grad_attended
    )
    key_send = jnp.concatenate([key_partial[:shard], key_partial[2 * shard :]], axis=0).astype(
        jnp.bfloat16
    )
    value_send = jnp.concatenate(
        [value_partial[:shard], value_partial[2 * shard :]], axis=0
    ).astype(jnp.bfloat16)
    key_got, value_got = rim(key_send, value_send, shard)
    grad_key = (
        key_partial[shard : 2 * shard]
        + key_got[:shard].astype(jnp.float32)
        + key_got[3 * shard :].astype(jnp.float32)
    ).astype(jnp.bfloat16)
    grad_value = (
        value_partial[shard : 2 * shard]
        + value_got[:shard].astype(jnp.float32)
        + value_got[3 * shard :].astype(jnp.float32)
    ).astype(jnp.bfloat16)
    grad_project = jnp.concatenate([grad_query, grad_key, grad_value], axis=1)
    grad_normed = jnp.dot(grad_project, full_qkv_space.T, preferred_element_type=jnp.float32)
    grad_in = (grad_stream.astype(jnp.float32) + rms_back(local_in, grad_normed)).astype(
        jnp.bfloat16
    )
    return (frames_out[None], grad_in[None])


def solution(mesh):
    in_specs = (
        P(("dp", "frame"), "space", None),
        P(("dp", "frame"), "space", None),
        P("space", None),
        P("space", None),
        P("space", None),
        P("space", None),
        P(),
    )
    out_specs = (P(("dp", "frame"), "space", None), P(("dp", "frame"), "space", None))
    return jax.shard_map(local, mesh=mesh, in_specs=in_specs, out_specs=out_specs, check_vma=False)
```

profile of v0, /device:TPU:64, one launch (start us, length us, event | category | flops | bytes accessed | tf_op | source)
XLA Modules:
  0.0 482.6 jit_solution(3111090518492652607)
XLA Ops:
  7.2 0.7 all-gather.11.cloned.1.call-update
  8.0 0.7 all-gather.5.cloned.1.call-update
  8.7 0.7 all-gather.7.cloned.1.call-update
  10.3 1.0 fusion.45
  11.4 0.6 multiply_multiply_fusion
  12.0 84.9 %all-gather.11.cloned.1.call-done = bf16[768,768]{1,0:T(8,128)(2,1)} async-done(((bf16[24,768]{1,0:T(8,128)(2,1)}), bf16[768,768]{1,0:T(8,128)(2,1)}) %all-gather.11.cloned.1.call-update) | async-done | bytes 1179664 | tf_op jit(solution)/shard_map/all_gather | solution.py:217
  96.9 1.9 fusion.37
  99.6 1.8 reduce.19
  101.5 0.7 reshape.405
  102.2 6.7 %all-to-all-start.2 = ((bf16[8,2,6144]{2,1,0:T(2,128)(2,1)}), bf16[8,2,6144]{2,1,0:T(2,128)(2,1)S(1)}, u32[]{:S(2)}, u32[]{:S(2)}) async-start(bf16[8,2,6144]{2,1,0:T(2,128)(2,1)} %reshape.405), calls=%async_computation.2 | async-start | bytes 393216 | tf_op jit(solution)/shard_map/all_to_all | solution.py:198
  108.9 75.4 %all-gather.5.cloned.1.call-done = bf16[768,2304]{1,0:T(8,128)(2,1)} async-done(((bf16[24,2304]{1,0:T(8,128)(2,1)}), bf16[768,2304]{1,0:T(8,128)(2,1)}) %all-gather.5.cloned.1.call-update) | async-done | bytes 3538960 | tf_op jit(solution)/shard_map/all_gather | solution.py:214
  184.4 2.7 convolution_convert_fusion.1
  187.1 3.6 collective-permute-start.1
  190.7 2.2 collective-permute-start
  192.9 5.7 %collective-permute-start.3 = (bf16[128,768]{1,0:T(8,128)(2,1)S(1)}, bf16[128,768]{1,0:T(8,128)(2,1)S(1)}, u32[]{:S(2)}, u32[]{:S(2)}) collective-permute-start(bf16[128,768]{1,0:T(8,128)(2,1)S(1)} %get-tuple-element.27), channel_id=1, source_target_pairs={{2,0},{4,2},{6,4},{8,6},{10,8},{12,10},{14,12},{16,14},{18,16},{20... | collective-permute-start | bytes 589832 | tf_op jit(solution)/shard_map/ppermute | solution.py:22
  198.7 2.1 collective-permute-start.2
  202.0 6.4 %collective-permute-done.2 = bf16[128,768]{1,0:T(8,128)(2,1)S(1)} collective-permute-done((bf16[128,768]{1,0:T(8,128)(2,1)S(1)}, bf16[128,768]{1,0:T(8,128)(2,1)S(1)}, u32[]{:S(2)}, u32[]{:S(2)}) %collective-permute-start.2) | collective-permute-done | bytes 196640 | tf_op jit(solution)/shard_map/ppermute | solution.py:20
  214.0 52.5 %all-gather.7.cloned.1.call-done = bf16[768,768]{1,0:T(8,128)(2,1)} async-done(((bf16[24,768]{1,0:T(8,128)(2,1)}), bf16[768,768]{1,0:T(8,128)(2,1)}) %all-gather.7.cloned.1.call-update) | async-done | bytes 1179664 | tf_op jit(solution)/shard_map/all_gather | solution.py:215
  266.5 1.7 multiply_reduce_fusion.2
  268.8 85.1 %all-gather.9.cloned.1.call-done = bf16[768,2304]{1,0:T(8,128)(2,1)} async-done(((bf16[24,2304]{1,0:T(8,128)(2,1)}), bf16[768,2304]{1,0:T(8,128)(2,1)}) %all-gather.9.cloned.1.call-update) | async-done | bytes 3538960 | tf_op jit(solution)/shard_map/all_gather | solution.py:216
  353.9 2.7 fusion
  356.6 0.9 copy.309
  357.5 4.4 reduce.20
  361.9 1.0 reshape.403
  362.8 6.7 %all-to-all-start = ((bf16[8,2,18432]{2,1,0:T(2,128)(2,1)}), bf16[8,2,18432]{2,1,0:T(2,128)(2,1)S(1)}, u32[]{:S(2)}, u32[]{:S(2)}) async-start(bf16[8,2,18432]{2,1,0:T(2,128)(2,1)} %reshape.403), calls=%async_computation | async-start | bytes 1179648 | tf_op jit(solution)/shard_map/all_to_all | solution.py:198
  370.3 1.1 bitcast_reduce_fusion
  372.3 1.1 fusion.86
  373.5 1.1 fusion.84
  374.6 10.4 %all-to-all-done = bf16[8,2,18432]{2,1,0:T(2,128)(2,1)S(1)} async-done(((bf16[8,2,18432]{2,1,0:T(2,128)(2,1)}), bf16[8,2,18432]{2,1,0:T(2,128)(2,1)S(1)}, u32[]{:S(2)}, u32[]{:S(2)}) %all-to-all-start) | async-done | bytes 589856 | tf_op jit(solution)/shard_map/all_to_all | solution.py:198
  385.0 0.6 reshape.404
  385.6 0.7 fusion.140
  387.0 1.5 fusion.2
  388.5 2.7 fusion.7
  391.2 2.5 fusion.57
  393.7 1.3 reshape.347
  395.0 3.1 multiply_reduce_fusion
  398.0 1.7 fusion.4
  400.9 1.0 reshape.350
  401.8 3.4 all-to-all-start.1
  406.5 0.9 pad_maximum_fusion.2
  407.4 7.5 %all-to-all-done.1 = bf16[8,16,768]{2,1,0:T(8,128)(2,1)S(1)} async-done(((bf16[8,16,768]{2,1,0:T(8,128)(2,1)}), bf16[8,16,768]{2,1,0:T(8,128)(2,1)S(1)}, u32[]{:S(2)}, u32[]{:S(2)}) %all-to-all-start.1) | async-done | bytes 196640 | tf_op jit(solution)/shard_map/all_to_all | solution.py:202
  414.9 4.5 all-to-all-start.3
  419.4 1.1 fusion.82
  420.6 1.1 fusion.80
  421.7 1.1 fusion.78
  422.7 2.2 fusion.76
  424.9 2.4 fusion.38
  427.3 5.8 %all-to-all-done.3 = bf16[8,16,2304]{2,1,0:T(8,128)(2,1)} async-done(((bf16[8,16,2304]{2,1,0:T(8,128)(2,1)}), bf16[8,16,2304]{2,1,0:T(8,128)(2,1)}, u32[]{:S(2)}, u32[]{:S(2)}) %all-to-all-start.3) | async-done | bytes 589856 | tf_op jit(solution)/shard_map/all_to_all | solution.py:202
  433.1 2.6 multiply_reduce_fusion.1
  436.0 1.1 copy-done.7
  443.2 1.4 fusion.103
  444.6 1.4 fusion.100
  446.0 1.4 fusion.97
  447.3 1.5 fusion.94
  448.8 1.4 fusion.91
  450.2 1.4 fusion.88
  451.8 3.6 collective-permute-start.5
  455.5 2.2 collective-permute-start.4
  458.0 6.0 %collective-permute-start.7 = (bf16[128,768]{0,1:T(8,128)(2,1)S(1)}, bf16[128,768]{0,1:T(8,128)(2,1)S(1)}, u32[]{:S(2)}, u32[]{:S(2)}) collective-permute-start(bf16[128,768]{0,1:T(8,128)(2,1)S(1)} %get-tuple-element.3), channel_id=1, source_target_pairs={{2,0},{4,2},{6,4},{8,6},{10,8},{12,10},{14,12},{16,14},{18,16},{20... | collective-permute-start | bytes 589832 | tf_op jit(solution)/shard_map/ppermute | solution.py:22
  464.0 1.9 collective-permute-start.6
  466.3 0.8 collective-permute-done.7
  467.1 6.5 %collective-permute-done.6 = bf16[128,768]{0,1:T(8,128)(2,1)S(1)} collective-permute-done((bf16[128,768]{0,1:T(8,128)(2,1)S(1)}, bf16[128,768]{0,1:T(8,128)(2,1)S(1)}, u32[]{:S(2)}, u32[]{:S(2)}) %collective-permute-start.6) | collective-permute-done | bytes 196640 | tf_op jit(solution)/shard_map/ppermute | solution.py:20
  473.8 1.4 fusion.51
  475.2 0.9 fusion.68
  (300 shorter events, 19.9 us)
Async XLA Ops:
  7.2 2.8 copy-start
  7.2 89.7 %all-gather.11.cloned.1.call-start = ((), (), s32[]{:S(2)}) async-start(), calls=%async_computation.7 | async-start | bytes 1216512 | tf_op jit(solution)/shard_map/all_gather | solution.py:217
  7.9 176.4 %all-gather.5.cloned.1.call-start = ((), (), s32[]{:S(2)}) async-start(), calls=%async_computation.4 | async-start | bytes 3649536 | tf_op jit(solution)/shard_map/all_gather | solution.py:214
  8.7 257.8 %all-gather.7.cloned.1.call-start = ((), (), s32[]{:S(2)}) async-start(), calls=%async_computation.5 | async-start | bytes 1216512 | tf_op jit(solution)/shard_map/all_gather | solution.py:215
  9.4 344.5 %all-gather.9.cloned.1.call-start = ((), (), s32[]{:S(2)}) async-start(), calls=%async_computation.6 | async-start | bytes 3649536 | tf_op jit(solution)/shard_map/all_gather | solution.py:216
  98.8 85.6 %copy-start.5 = (bf16[1,128,768]{2,1,0:T(8,128)(2,1)S(1)}, bf16[1,128,768]{2,1,0:T(8,128)(2,1)}, u32[]{:S(2)}) copy-start(bf16[1,128,768]{2,1,0:T(8,128)(2,1)} %param.7) | copy-start | bytes 589828
  102.2 260.6 %all-to-all-start.2 = ((bf16[8,2,6144]{2,1,0:T(2,128)(2,1)}), bf16[8,2,6144]{2,1,0:T(2,128)(2,1)S(1)}, u32[]{:S(2)}, u32[]{:S(2)}) async-start(bf16[8,2,6144]{2,1,0:T(2,128)(2,1)} %reshape.405), calls=%async_computation.2 | async-start | bytes 393216 | tf_op jit(solution)/shard_map/all_to_all | solution.py:198
  187.1 14.5 %collective-permute-start.1 = (bf16[128,768]{1,0:T(8,128)(2,1)S(1)}, bf16[128,768]{1,0:T(8,128)(2,1)S(1)}, u32[]{:S(2)}, u32[]{:S(2)}) collective-permute-start(bf16[128,768]{1,0:T(8,128)(2,1)S(1)} %get-tuple-element.28), channel_id=1, source_target_pairs={{2,0},{4,2},{6,4},{8,6},{10,8},{12,10},{14,12},{16,14},{18,16},{20... | collective-permute-start | bytes 589832 | tf_op jit(solution)/shard_map/ppermute | solution.py:22
  190.7 10.9 %collective-permute-start = (bf16[128,768]{1,0:T(8,128)(2,1)S(1)}, bf16[128,768]{1,0:T(8,128)(2,1)S(1)}, u32[]{:S(2)}, u32[]{:S(2)}) collective-permute-start(bf16[128,768]{1,0:T(8,128)(2,1)S(1)} %get-tuple-element.28), channel_id=1, source_target_pairs={{0,2},{2,4},{4,6},{6,8},{8,10},{10,12},{12,14},{14,16},{16,18},{18... | collective-permute-start | bytes 589832 | tf_op jit(solution)/shard_map/ppermute | solution.py:20
  192.9 9.1 %collective-permute-start.3 = (bf16[128,768]{1,0:T(8,128)(2,1)S(1)}, bf16[128,768]{1,0:T(8,128)(2,1)S(1)}, u32[]{:S(2)}, u32[]{:S(2)}) collective-permute-start(bf16[128,768]{1,0:T(8,128)(2,1)S(1)} %get-tuple-element.27), channel_id=1, source_target_pairs={{2,0},{4,2},{6,4},{8,6},{10,8},{12,10},{14,12},{16,14},{18,16},{20... | collective-permute-start | bytes 589832 | tf_op jit(solution)/shard_map/ppermute | solution.py:22
  198.7 9.8 %collective-permute-start.2 = (bf16[128,768]{1,0:T(8,128)(2,1)S(1)}, bf16[128,768]{1,0:T(8,128)(2,1)S(1)}, u32[]{:S(2)}, u32[]{:S(2)}) collective-permute-start(bf16[128,768]{1,0:T(8,128)(2,1)S(1)} %get-tuple-element.27), channel_id=1, source_target_pairs={{0,2},{2,4},{4,6},{6,8},{8,10},{10,12},{12,14},{14,16},{16,18},{18... | collective-permute-start | bytes 589832 | tf_op jit(solution)/shard_map/ppermute | solution.py:20
  200.9 9.2 %copy-start.65 = (bf16[128,128]{0,1:T(8,128)(2,1)}, bf16[128,128]{0,1:T(8,128)(2,1)S(1)}, u32[]{:S(2)}) copy-start(bf16[128,128]{0,1:T(8,128)(2,1)S(1)} %copy.184) | copy-start | bytes 98308
  201.1 9.7 %copy-start.62 = (bf16[128,128]{0,1:T(8,128)(2,1)}, bf16[128,128]{0,1:T(8,128)(2,1)S(1)}, u32[]{:S(2)}) copy-start(bf16[128,128]{0,1:T(8,128)(2,1)S(1)} %copy.187) | copy-start | bytes 98308
  201.2 10.2 %copy-start.59 = (bf16[128,128]{0,1:T(8,128)(2,1)}, bf16[128,128]{0,1:T(8,128)(2,1)S(1)}, u32[]{:S(2)}) copy-start(bf16[128,128]{0,1:T(8,128)(2,1)S(1)} %copy.190) | copy-start | bytes 98308
  201.3 10.7 %copy-start.56 = (bf16[128,128]{0,1:T(8,128)(2,1)}, bf16[128,128]{0,1:T(8,128)(2,1)S(1)}, u32[]{:S(2)}) copy-start(bf16[128,128]{0,1:T(8,128)(2,1)S(1)} %copy.193) | copy-start | bytes 98308
  201.5 11.3 %copy-start.53 = (bf16[128,128]{0,1:T(8,128)(2,1)}, bf16[128,128]{0,1:T(8,128)(2,1)S(1)}, u32[]{:S(2)}) copy-start(bf16[128,128]{0,1:T(8,128)(2,1)S(1)} %copy.196) | copy-start | bytes 98308
  201.6 11.8 %copy-start.51 = (bf16[128,128]{0,1:T(8,128)(2,1)}, bf16[128,128]{0,1:T(8,128)(2,1)S(1)}, u32[]{:S(2)}) copy-start(bf16[128,128]{0,1:T(8,128)(2,1)S(1)} %copy.199) | copy-start | bytes 98308
  201.9 8.5 %copy-start.45 = (bf16[384,128]{0,1:T(8,128)(2,1)}, bf16[384,128]{0,1:T(8,128)(2,1)S(1)}, u32[]{:S(2)}) copy-start(bf16[384,128]{0,1:T(8,128)(2,1)S(1)} %copy.183) | copy-start | bytes 294916
  208.7 1.7 copy-start.20
  208.9 2.2 copy-start.49
  209.0 1.8 copy-start.17
  209.2 2.6 copy-start.47
  209.3 2.1 copy-start.14
  209.4 2.9 copy-start.43
  209.6 211.0 %copy-start.12 = (bf16[384,128]{0,1:T(8,128)(2,1)}, bf16[384,128]{0,1:T(8,128)(2,1)S(1)}, u32[]{:S(2)}) copy-start(bf16[384,128]{0,1:T(8,128)(2,1)S(1)} %copy.194) | copy-start | bytes 294916
  209.7 3.3 copy-start.41
  209.8 211.8 %copy-start.10 = (bf16[384,128]{0,1:T(8,128)(2,1)}, bf16[384,128]{0,1:T(8,128)(2,1)S(1)}, u32[]{:S(2)}) copy-start(bf16[384,128]{0,1:T(8,128)(2,1)S(1)} %copy.197) | copy-start | bytes 294916
  210.0 3.7 copy-start.39
  210.1 3.2 copy-start.8
  213.3 54.9 %copy-start.70 = (bf16[2,64,128]{2,1,0:T(8,128)(2,1)}, bf16[2,64,128]{2,1,0:T(8,128)(2,1)S(1)}, u32[]{:S(2)}) copy-start(bf16[2,64,128]{2,1,0:T(8,128)(2,1)S(1)} %convolution_convert_fusion.7) | copy-start | bytes 98308
  213.7 54.6 %copy-start.32 = (f32[2,128,384]{2,1,0:T(8,128)}, f32[2,128,384]{2,1,0:T(8,128)S(1)}, u32[]{:S(2)}) copy-start(f32[2,128,384]{2,1,0:T(8,128)S(1)} %fusion.21) | copy-start | bytes 1179652
  214.0 142.6 %copy-start.68 = (bf16[2,64,128]{2,1,0:T(8,128)(2,1)}, bf16[2,64,128]{2,1,0:T(8,128)(2,1)S(1)}, u32[]{:S(2)}) copy-start(bf16[2,64,128]{2,1,0:T(8,128)(2,1)S(1)} %convolution_convert_fusion.6) | copy-start | bytes 98308
  268.3 88.3 %copy-start.3 = (f32[128,768]{1,0:T(8,128)}, f32[128,768]{1,0:T(8,128)S(1)}, u32[]{:S(2)}) copy-start(f32[128,768]{1,0:T(8,128)S(1)} %get-tuple-element.40) | copy-start | bytes 1179652
  362.8 22.1 %all-to-all-start = ((bf16[8,2,18432]{2,1,0:T(2,128)(2,1)}), bf16[8,2,18432]{2,1,0:T(2,128)(2,1)S(1)}, u32[]{:S(2)}, u32[]{:S(2)}) async-start(bf16[8,2,18432]{2,1,0:T(2,128)(2,1)} %reshape.403), calls=%async_computation | async-start | bytes 1179648 | tf_op jit(solution)/shard_map/all_to_all | solution.py:198
  400.6 4.6 copy-start.25
  401.8 13.1 %all-to-all-start.1 = ((bf16[8,16,768]{2,1,0:T(8,128)(2,1)}), bf16[8,16,768]{2,1,0:T(8,128)(2,1)S(1)}, u32[]{:S(2)}, u32[]{:S(2)}) async-start(bf16[8,16,768]{2,1,0:T(8,128)(2,1)} %reshape.350), calls=%async_computation.1 | async-start | bytes 393216 | tf_op jit(solution)/shard_map/all_to_all | solution.py:202
  406.5 12.9 %copy-start.15 = (bf16[384,128]{0,1:T(8,128)(2,1)S(1)}, bf16[384,128]{0,1:T(8,128)(2,1)}, u32[]{:S(2)}) copy-start(bf16[384,128]{0,1:T(8,128)(2,1)} %copy-done.14) | copy-start | bytes 294916
  406.5 12.9 %copy-start.60 = (bf16[128,128]{0,1:T(8,128)(2,1)S(1)}, bf16[128,128]{0,1:T(8,128)(2,1)}, u32[]{:S(2)}) copy-start(bf16[128,128]{0,1:T(8,128)(2,1)} %copy-done.59) | copy-start | bytes 98308
  414.9 5.6 %copy-start.24 = (bf16[8,16,768]{2,1,0:T(8,128)(2,1)}, bf16[8,16,768]{2,1,0:T(8,128)(2,1)S(1)}, u32[]{:S(2)}) copy-start(bf16[8,16,768]{2,1,0:T(8,128)(2,1)S(1)} %all-to-all-done.1) | copy-start | bytes 589828
  414.9 18.2 %all-to-all-start.3 = ((bf16[8,16,2304]{2,1,0:T(8,128)(2,1)}), bf16[8,16,2304]{2,1,0:T(8,128)(2,1)}, u32[]{:S(2)}, u32[]{:S(2)}) async-start(bf16[8,16,2304]{2,1,0:T(8,128)(2,1)} %pad_maximum_fusion.2), calls=%async_computation.3 | async-start | bytes 1179648 | tf_op jit(solution)/shard_map/all_to_all | solution.py:202
  422.7 10.4 %copy-start.2 = (bf16[768,2304]{1,0:T(8,128)(2,1)S(1)}, bf16[768,2304]{1,0:T(8,128)(2,1)}, u32[]{:S(2)}) copy-start(bf16[768,2304]{1,0:T(8,128)(2,1)} %all-gather.9.cloned.1.call-done) | copy-start | bytes 10616836
  433.1 2.6 copy-start.4
  433.1 2.7 copy-start.23
  433.1 2.7 copy-start.80
  438.3 1.5 copy-start.75
  438.3 1.5 copy-start.38
  438.4 1.5 copy-start.48
  439.0 1.4 copy-start.61
  439.2 1.5 copy-start.73
  439.2 1.5 copy-start.37
  439.3 1.5 copy-start.44
  439.9 1.4 copy-start.58
  440.1 1.5 copy-start.71
  440.1 1.5 copy-start.36
  440.2 1.5 copy-start.42
  441.0 1.4 copy-start.69
  441.1 1.5 copy-start.35
  441.1 1.4 copy-start.40
  451.8 14.2 %collective-permute-start.5 = (bf16[128,768]{0,1:T(8,128)(2,1)S(1)}, bf16[128,768]{0,1:T(8,128)(2,1)S(1)}, u32[]{:S(2)}, u32[]{:S(2)}) collective-permute-start(bf16[128,768]{0,1:T(8,128)(2,1)S(1)} %get-tuple-element.5), channel_id=1, source_target_pairs={{2,0},{4,2},{6,4},{8,6},{10,8},{12,10},{14,12},{16,14},{18,16},{20... | collective-permute-start | bytes 589832 | tf_op jit(solution)/shard_map/ppermute | solution.py:22
  455.5 10.8 %collective-permute-start.4 = (bf16[128,768]{0,1:T(8,128)(2,1)S(1)}, bf16[128,768]{0,1:T(8,128)(2,1)S(1)}, u32[]{:S(2)}, u32[]{:S(2)}) collective-permute-start(bf16[128,768]{0,1:T(8,128)(2,1)S(1)} %get-tuple-element.4), channel_id=1, source_target_pairs={{0,2},{2,4},{4,6},{6,8},{8,10},{10,12},{12,14},{14,16},{16,18},{18... | collective-permute-start | bytes 589832 | tf_op jit(solution)/shard_map/ppermute | solution.py:20
  457.8 15.9 %copy-start.1 = (bf16[768,2304]{1,0:T(8,128)(2,1)S(1)}, bf16[768,2304]{1,0:T(8,128)(2,1)}, u32[]{:S(2)}) copy-start(bf16[768,2304]{1,0:T(8,128)(2,1)} %all-gather.5.cloned.1.call-done) | copy-start | bytes 10616836
  458.0 15.8 %copy-start.6 = (bf16[1,128,768]{2,1,0:T(8,128)(2,1)S(1)}, bf16[1,128,768]{2,1,0:T(8,128)(2,1)}, u32[]{:S(2)}) copy-start(bf16[1,128,768]{2,1,0:T(8,128)(2,1)} %param.7) | copy-start | bytes 589828
  458.0 9.2 %collective-permute-start.7 = (bf16[128,768]{0,1:T(8,128)(2,1)S(1)}, bf16[128,768]{0,1:T(8,128)(2,1)S(1)}, u32[]{:S(2)}, u32[]{:S(2)}) collective-permute-start(bf16[128,768]{0,1:T(8,128)(2,1)S(1)} %get-tuple-element.3), channel_id=1, source_target_pairs={{2,0},{4,2},{6,4},{8,6},{10,8},{12,10},{14,12},{16,14},{18,16},{20... | collective-permute-start | bytes 589832 | tf_op jit(solution)/shard_map/ppermute | solution.py:22
  464.0 9.7 %collective-permute-start.6 = (bf16[128,768]{0,1:T(8,128)(2,1)S(1)}, bf16[128,768]{0,1:T(8,128)(2,1)S(1)}, u32[]{:S(2)}, u32[]{:S(2)}) collective-permute-start(bf16[128,768]{0,1:T(8,128)(2,1)S(1)} %get-tuple-element.2), channel_id=1, source_target_pairs={{0,2},{2,4},{4,6},{6,8},{8,10},{10,12},{12,14},{14,16},{16,18},{18... | collective-permute-start | bytes 589832 | tf_op jit(solution)/shard_map/ppermute | solution.py:20
  (35 other events, 39.5 us)
Sparse Core Ops, SparseCore 0:
  11.2 85.5 all-gather.10
  100.0 84.2 all-gather.4
  187.6 78.8 all-gather.6
  269.5 84.2 all-gather.8
where the time goes:
time: 484 us; the launch traced here: 483 us
  waiting for transfers between devices  338 us (70%)
  starting transfers between devices  48.9 us (10%)
  matrix products  48.9 us (10%)
  local copies, waits for them, and re-layouts  16.5 us (3%)
  between operations  15.8 us (3%)
  other arithmetic  14.1 us (3%)
    all_gather x1, waiting for transfers between devices, local(): lax.all_gather(w_qkv_time, 'space', axis=0, tiled=True)  85.1 us
    all_gather x1, waiting for transfers between devices, local(): lax.all_gather(w_out_time, 'space', axis=0, tiled=True)  84.9 us
    all_gather x1, waiting for transfers between devices, local(): lax.all_gather(w_qkv_space, 'space', axis=0, tiled=True)  75.4 us
    all_gather x1, waiting for transfers between devices, local(): lax.all_gather(w_out_space, 'space', axis=0, tiled=True)  52.5 us
    ppermute x4, starting transfers between devices, padded(): lax.ppermute(head, axis, [((i + 1) % count, i) for i in range(ends)])  19 us
    all_to_all x2, starting transfers between devices, to_frames(): lax.all_to_all(local_rows[None], 'frame', split_axis=1, concat_axis=0, ti...  13.5 us
    all_to_all x2, waiting for transfers between devices, to_space(): lax.all_to_all(frame_rows, 'frame', split_axis=0, concat_axis=1, tiled=True)  13.3 us
    ppermute x4, waiting for transfers between devices, padded(): lax.ppermute(tail, axis, [(i, (i + 1) % count) for i in range(ends)])  13.2 us
  transfers between devices with their start and end apart: 16, of which 12 were waited for; matrix products, arithmetic and copies ran while one was open for 9% of the time, Pallas kernels for 0%

commit v1 on v0

--- a/solution.py
+++ b/solution.py
@@ -1,3 +1,4 @@
+import functools
 import jax
 import jax.numpy as jnp
 from jax import lax
@@ -7,6 +8,19 @@
 HD = 64
 BLOCK = 128
 EPS = 1e-06
+
+
+def draft_signs_up(incoming_x, across):
+    return lax.all_to_all(
+        jnp.concatenate(tuple((incoming_x for _ in range(lax.axis_size(across)))), 0),
+        axis_name=across,
+        split_axis=0,
+        concat_axis=0,
+        tiled=True,
+    )
+
+
+order_roots = functools.partial(draft_signs_up, across="space")
 
 
 def padded(cells, sides, width):
@@ -214,7 +228,7 @@
         lax.all_gather(w_qkv_space, "space", axis=0, tiled=True),
         lax.all_gather(w_out_space, "space", axis=0, tiled=True),
         lax.all_gather(w_qkv_time, "space", axis=0, tiled=True),
-        lax.all_gather(w_out_time, "space", axis=0, tiled=True),
+        order_roots(w_out_time),
     )
     block_count = shard // BLOCK
     space_index = lax.axis_index("space")

time: 484 us -> 406 us (0.84)
  waiting for transfers between devices: 338 us -> 218 us
  local copies, waits for them, and re-layouts: 16.5 us -> 46.2 us
  starting transfers between devices: 48.9 us -> 63.1 us
    all_gather x1 -> x0, waiting for transfers between devices: 84.9 us -> none  [local(): lax.all_gather(w_out_time, 'space', axis=0, tiled=True)]
    all_gather x1, waiting for transfers between devices: 75.4 us -> 8.31 us  [local(): lax.all_gather(w_qkv_space, 'space', axis=0, tiled=True)]
    all_to_all x0 -> x1, waiting for transfers between devices: none -> 31.3 us  [draft_signs_up(): lax.all_to_all(jnp.concatenate(tuple((incoming_x for _ in range(lax.axis_...]
    unnamed x193 -> x226, local copies, waits for them, and re-layouts: 5.5 us -> 36 us
    all_to_all x0 -> x1, starting transfers between devices: none -> 12.7 us  [draft_signs_up(): lax.all_to_all(jnp.concatenate(tuple((incoming_x for _ in range(lax.axis_...]
  transfers between devices with their start and end apart: 16 -> 16, of which waited for: 12 -> 11; matrix products, arithmetic and copies ran while one was open for 9% -> 17% of each run, Pallas kernels for 0% -> 0%
where the time goes in v1:
time: 406 us; the launch traced here: 404 us
  waiting for transfers between devices  218 us (54%)
  starting transfers between devices  63.1 us (16%)
  matrix products  47.5 us (12%)
  local copies, waits for them, and re-layouts  46.2 us (11%)
  between operations  15.8 us (4%)
  other arithmetic  13.2 us (3%)
    all_gather x1, waiting for transfers between devices, local(): lax.all_gather(w_qkv_time, 'space', axis=0, tiled=True)  85.2 us
    all_gather x1, waiting for transfers between devices, local(): lax.all_gather(w_out_space, 'space', axis=0, tiled=True)  53.3 us
    unnamed x226, local copies, waits for them, and re-layouts  36 us
    all_to_all x1, waiting for transfers between devices, draft_signs_up(): lax.all_to_all(jnp.concatenate(tuple((incoming_x for _ in range(lax.axis_...  31.3 us
    ppermute x4, starting transfers between devices, padded(): lax.ppermute(head, axis, [((i + 1) % count, i) for i in range(ends)])  20.4 us
    all_to_all x2, starting transfers between devices, to_frames(): lax.all_to_all(local_rows[None], 'frame', split_axis=1, concat_axis=0, ti...  13.8 us
    all_to_all x2, waiting for transfers between devices, to_space(): lax.all_to_all(frame_rows, 'frame', split_axis=0, concat_axis=1, tiled=True)  13.3 us
    ppermute x4, waiting for transfers between devices, padded(): lax.ppermute(tail, axis, [(i, (i + 1) % count) for i in range(ends)])  13.2 us
  transfers between devices with their start and end apart: 16, of which 11 were waited for; matrix products, arithmetic and copies ran while one was open for 17% of the time, Pallas kernels for 0%

profile of v1, /device:TPU:64, one launch (start us, length us, event | category | flops | bytes accessed | tf_op | source)
XLA Modules:
  0.0 403.8 jit_solution(14815984744040046977)
XLA Ops:
  8.7 1.4 constant_dynamic-update-slice_fusion.37
  10.1 1.4 constant_dynamic-update-slice_fusion.36
  11.4 1.4 constant_dynamic-update-slice_fusion.35
  12.8 1.4 constant_dynamic-update-slice_fusion.34
  14.2 1.4 constant_dynamic-update-slice_fusion.33
  15.6 1.4 constant_dynamic-update-slice_fusion.32
  17.0 1.4 constant_dynamic-update-slice_fusion.31
  18.3 1.4 constant_dynamic-update-slice_fusion.30
  19.7 1.4 constant_dynamic-update-slice_fusion.29
  21.1 1.4 constant_dynamic-update-slice_fusion.28
  22.5 1.4 constant_dynamic-update-slice_fusion.27
  23.9 1.4 constant_dynamic-update-slice_fusion.26
  25.3 1.4 constant_dynamic-update-slice_fusion.25
  26.6 1.4 constant_dynamic-update-slice_fusion.24
  39.1 12.7 %all-to-all-start.2 = ((bf16[32,24,768]{2,1,0:T(8,128)(2,1)}), bf16[32,24,768]{2,1,0:T(8,128)(2,1)S(1)}, u32[]{:S(2)}, u32[]{:S(2)}) async-start(bf16[32,24,768]{2,1,0:T(8,128)(2,1)} %bitcast.50), calls=%async_computation.2 | async-start | bytes 2359296 | tf_op jit(solution)/shard_map/all_to_all | solution.py:14
  53.6 31.3 %all-to-all-done.2 = bf16[32,24,768]{2,1,0:T(8,128)(2,1)S(1)} async-done(((bf16[32,24,768]{2,1,0:T(8,128)(2,1)}), bf16[32,24,768]{2,1,0:T(8,128)(2,1)S(1)}, u32[]{:S(2)}, u32[]{:S(2)}) %all-to-all-start.2) | async-done | bytes 1179680 | tf_op jit(solution)/shard_map/all_to_all | solution.py:14
  86.4 1.8 reduce.19
  89.0 7.0 %all-to-all-start.3 = ((bf16[8,2,6144]{2,1,0:T(2,128)(2,1)}), bf16[8,2,6144]{2,1,0:T(2,128)(2,1)S(1)}, u32[]{:S(2)}, u32[]{:S(2)}) async-start(bf16[8,2,6144]{2,1,0:T(2,128)(2,1)} %reshape.407), calls=%async_computation.3 | async-start | bytes 393216 | tf_op jit(solution)/shard_map/all_to_all | solution.py:212
  96.0 8.3 %all-gather.4.cloned.1.call-done = bf16[768,2304]{1,0:T(8,128)(2,1)} async-done(((bf16[24,2304]{1,0:T(8,128)(2,1)}), bf16[768,2304]{1,0:T(8,128)(2,1)}) %all-gather.4.cloned.1.call-update) | async-done | bytes 3538960 | tf_op jit(solution)/shard_map/all_gather | solution.py:228
  104.3 2.7 convolution_convert_fusion.1
  107.0 4.8 %collective-permute-start.1 = (bf16[128,768]{1,0:T(8,128)(2,1)S(1)}, bf16[128,768]{1,0:T(8,128)(2,1)S(1)}, u32[]{:S(2)}, u32[]{:S(2)}) collective-permute-start(bf16[128,768]{1,0:T(8,128)(2,1)S(1)} %get-tuple-element.28), channel_id=1, source_target_pairs={{2,0},{4,2},{6,4},{8,6},{10,8},{12,10},{14,12},{16,14},{18,16},{20... | collective-permute-start | bytes 589832 | tf_op jit(solution)/shard_map/ppermute | solution.py:36
  111.9 1.9 collective-permute-start
  113.8 6.0 %collective-permute-start.3 = (bf16[128,768]{1,0:T(8,128)(2,1)S(1)}, bf16[128,768]{1,0:T(8,128)(2,1)S(1)}, u32[]{:S(2)}, u32[]{:S(2)}) collective-permute-start(bf16[128,768]{1,0:T(8,128)(2,1)S(1)} %get-tuple-element.27), channel_id=1, source_target_pairs={{2,0},{4,2},{6,4},{8,6},{10,8},{12,10},{14,12},{16,14},{18,16},{20... | collective-permute-start | bytes 589832 | tf_op jit(solution)/shard_map/ppermute | solution.py:36
  119.8 2.1 collective-permute-start.2
  123.1 6.5 %collective-permute-done.2 = bf16[128,768]{1,0:T(8,128)(2,1)S(1)} collective-permute-done((bf16[128,768]{1,0:T(8,128)(2,1)S(1)}, bf16[128,768]{1,0:T(8,128)(2,1)S(1)}, u32[]{:S(2)}, u32[]{:S(2)}) %collective-permute-start.2) | collective-permute-done | bytes 196640 | tf_op jit(solution)/shard_map/ppermute | solution.py:34
  135.9 53.3 %all-gather.6.cloned.1.call-done = bf16[768,768]{1,0:T(8,128)(2,1)} async-done(((bf16[24,768]{1,0:T(8,128)(2,1)}), bf16[768,768]{1,0:T(8,128)(2,1)}) %all-gather.6.cloned.1.call-update) | async-done | bytes 1179664 | tf_op jit(solution)/shard_map/all_gather | solution.py:229
  189.2 1.7 multiply_reduce_fusion.2
  191.5 85.2 %all-gather.8.cloned.1.call-done = bf16[768,2304]{1,0:T(8,128)(2,1)} async-done(((bf16[24,2304]{1,0:T(8,128)(2,1)}), bf16[768,2304]{1,0:T(8,128)(2,1)}) %all-gather.8.cloned.1.call-update) | async-done | bytes 3538960 | tf_op jit(solution)/shard_map/all_gather | solution.py:230
  276.7 2.7 fusion
  280.3 4.4 %reduce.20 = bf16[128,2304]{1,0:T(8,128)(2,1)S(1)} reduce(bf16[128,1,2304]{2,1,0:T(2,128)(2,1)S(1)} %bitcast.298, bf16[]{:T(256)} %broadcast.211), dimensions={1}, to_apply=%bitcast.295.reduce_sub_computation | reduce | bytes 1179650
  285.7 6.7 %all-to-all-start = ((bf16[8,2,18432]{2,1,0:T(2,128)(2,1)}), bf16[8,2,18432]{2,1,0:T(2,128)(2,1)S(1)}, u32[]{:S(2)}, u32[]{:S(2)}) async-start(bf16[8,2,18432]{2,1,0:T(2,128)(2,1)} %reshape.405), calls=%async_computation | async-start | bytes 1179648 | tf_op jit(solution)/shard_map/all_to_all | solution.py:212
  293.2 1.1 bitcast_reduce_fusion
  295.0 1.1 fusion.86
  296.2 1.1 fusion.84
  297.3 10.5 %all-to-all-done = bf16[8,2,18432]{2,1,0:T(2,128)(2,1)S(1)} async-done(((bf16[8,2,18432]{2,1,0:T(2,128)(2,1)}), bf16[8,2,18432]{2,1,0:T(2,128)(2,1)S(1)}, u32[]{:S(2)}, u32[]{:S(2)}) %all-to-all-start) | async-done | bytes 589856 | tf_op jit(solution)/shard_map/all_to_all | solution.py:212
  309.2 1.5 fusion.2
  310.7 2.7 fusion.7
  313.4 2.5 fusion.57
  316.2 3.1 multiply_reduce_fusion
  319.3 1.7 fusion.4
  322.1 1.0 reshape.352
  323.1 3.4 all-to-all-start.1
  328.6 7.5 %all-to-all-done.1 = bf16[8,16,768]{2,1,0:T(8,128)(2,1)S(1)} async-done(((bf16[8,16,768]{2,1,0:T(8,128)(2,1)}), bf16[8,16,768]{2,1,0:T(8,128)(2,1)S(1)}, u32[]{:S(2)}, u32[]{:S(2)}) %all-to-all-start.1) | async-done | bytes 196640 | tf_op jit(solution)/shard_map/all_to_all | solution.py:216
  336.2 4.5 %all-to-all-start.4 = ((bf16[8,16,2304]{2,1,0:T(8,128)(2,1)}), bf16[8,16,2304]{2,1,0:T(8,128)(2,1)}, u32[]{:S(2)}, u32[]{:S(2)}) async-start(bf16[8,16,2304]{2,1,0:T(8,128)(2,1)} %pad_maximum_fusion.2), calls=%async_computation.4 | async-start | bytes 1179648 | tf_op jit(solution)/shard_map/all_to_all | solution.py:216
  340.7 1.1 fusion.82
  341.8 1.1 fusion.80
  342.9 1.1 fusion.78
  344.0 2.2 fusion.76
  346.2 2.4 fusion.38
  348.6 5.8 %all-to-all-done.4 = bf16[8,16,2304]{2,1,0:T(8,128)(2,1)} async-done(((bf16[8,16,2304]{2,1,0:T(8,128)(2,1)}), bf16[8,16,2304]{2,1,0:T(8,128)(2,1)}, u32[]{:S(2)}, u32[]{:S(2)}) %all-to-all-start.4) | async-done | bytes 589856 | tf_op jit(solution)/shard_map/all_to_all | solution.py:216
  354.4 2.6 multiply_reduce_fusion.1
  357.2 1.1 copy-done.9
  364.5 1.4 fusion.103
  365.8 1.4 fusion.100
  367.2 1.4 fusion.97
  368.6 1.5 fusion.94
  370.1 1.4 fusion.91
  371.5 1.4 fusion.88
  373.1 3.6 collective-permute-start.5
  376.7 2.2 collective-permute-start.4
  379.2 6.0 %collective-permute-start.7 = (bf16[128,768]{0,1:T(8,128)(2,1)S(1)}, bf16[128,768]{0,1:T(8,128)(2,1)S(1)}, u32[]{:S(2)}, u32[]{:S(2)}) collective-permute-start(bf16[128,768]{0,1:T(8,128)(2,1)S(1)} %get-tuple-element.3), channel_id=1, source_target_pairs={{2,0},{4,2},{6,4},{8,6},{10,8},{12,10},{14,12},{16,14},{18,16},{20... | collective-permute-start | bytes 589832 | tf_op jit(solution)/shard_map/ppermute | solution.py:36
  385.2 1.9 collective-permute-start.6
  388.4 6.5 %collective-permute-done.6 = bf16[128,768]{0,1:T(8,128)(2,1)S(1)} collective-permute-done((bf16[128,768]{0,1:T(8,128)(2,1)S(1)}, bf16[128,768]{0,1:T(8,128)(2,1)S(1)}, u32[]{:S(2)}, u32[]{:S(2)}) %collective-permute-start.6) | collective-permute-done | bytes 196640 | tf_op jit(solution)/shard_map/ppermute | solution.py:34
  395.0 1.4 fusion.51
  (333 shorter events, 40.5 us)
Async XLA Ops:
  7.2 45.4 %copy-start = (s32[32,4]{0,1:T(4,128)S(1)}, s32[32,4]{0,1:T(4,128)}, u32[]{:S(2)}) copy-start(s32[32,4]{0,1:T(4,128)} %param.13) | copy-start | bytes 1540
  7.2 20.8 %copy-start.1 = (bf16[24,768]{1,0:T(8,128)(2,1)S(1)}, bf16[24,768]{1,0:T(8,128)(2,1)}, u32[]{:S(2)}) copy-start(bf16[24,768]{1,0:T(8,128)(2,1)} %param.12) | copy-start | bytes 110596
  7.2 97.1 %all-gather.4.cloned.1.call-start = ((), (), s32[]{:S(2)}) async-start(), calls=%async_computation.5 | async-start | bytes 3649536 | tf_op jit(solution)/shard_map/all_gather | solution.py:228
  7.9 181.3 %all-gather.6.cloned.1.call-start = ((), (), s32[]{:S(2)}) async-start(), calls=%async_computation.6 | async-start | bytes 1216512 | tf_op jit(solution)/shard_map/all_gather | solution.py:229
  39.1 13.8 %copy-start.7 = (bf16[1,128,768]{2,1,0:T(8,128)(2,1)S(1)}, bf16[1,128,768]{2,1,0:T(8,128)(2,1)}, u32[]{:S(2)}) copy-start(bf16[1,128,768]{2,1,0:T(8,128)(2,1)} %param.7) | copy-start | bytes 589828
  39.1 45.9 %copy-start.23 = (bf16[1,128,768]{2,1,0:T(8,128)(2,1)S(1)}, bf16[1,128,768]{2,1,0:T(8,128)(2,1)}, u32[]{:S(2)}) copy-start(bf16[1,128,768]{2,1,0:T(8,128)(2,1)} %param.8) | copy-start | bytes 589828
  39.1 45.9 %all-to-all-start.2 = ((bf16[32,24,768]{2,1,0:T(8,128)(2,1)}), bf16[32,24,768]{2,1,0:T(8,128)(2,1)S(1)}, u32[]{:S(2)}, u32[]{:S(2)}) async-start(bf16[32,24,768]{2,1,0:T(8,128)(2,1)} %bitcast.50), calls=%async_computation.2 | async-start | bytes 2359296 | tf_op jit(solution)/shard_map/all_to_all | solution.py:14
  51.8 224.9 %all-gather.8.cloned.1.call-start = ((), (), s32[]{:S(2)}) async-start(), calls=%async_computation.7 | async-start | bytes 3649536 | tf_op jit(solution)/shard_map/all_gather | solution.py:230
  85.0 3.3 copy-start.4
  89.0 196.7 %all-to-all-start.3 = ((bf16[8,2,6144]{2,1,0:T(2,128)(2,1)}), bf16[8,2,6144]{2,1,0:T(2,128)(2,1)S(1)}, u32[]{:S(2)}, u32[]{:S(2)}) async-start(bf16[8,2,6144]{2,1,0:T(2,128)(2,1)} %reshape.407), calls=%async_computation.3 | async-start | bytes 393216 | tf_op jit(solution)/shard_map/all_to_all | solution.py:212
  107.0 15.7 %collective-permute-start.1 = (bf16[128,768]{1,0:T(8,128)(2,1)S(1)}, bf16[128,768]{1,0:T(8,128)(2,1)S(1)}, u32[]{:S(2)}, u32[]{:S(2)}) collective-permute-start(bf16[128,768]{1,0:T(8,128)(2,1)S(1)} %get-tuple-element.28), channel_id=1, source_target_pairs={{2,0},{4,2},{6,4},{8,6},{10,8},{12,10},{14,12},{16,14},{18,16},{20... | collective-permute-start | bytes 589832 | tf_op jit(solution)/shard_map/ppermute | solution.py:36
  111.9 10.9 %collective-permute-start = (bf16[128,768]{1,0:T(8,128)(2,1)S(1)}, bf16[128,768]{1,0:T(8,128)(2,1)S(1)}, u32[]{:S(2)}, u32[]{:S(2)}) collective-permute-start(bf16[128,768]{1,0:T(8,128)(2,1)S(1)} %get-tuple-element.28), channel_id=1, source_target_pairs={{0,2},{2,4},{4,6},{6,8},{8,10},{10,12},{12,14},{14,16},{16,18},{18... | collective-permute-start | bytes 589832 | tf_op jit(solution)/shard_map/ppermute | solution.py:34
  113.8 9.3 %collective-permute-start.3 = (bf16[128,768]{1,0:T(8,128)(2,1)S(1)}, bf16[128,768]{1,0:T(8,128)(2,1)S(1)}, u32[]{:S(2)}, u32[]{:S(2)}) collective-permute-start(bf16[128,768]{1,0:T(8,128)(2,1)S(1)} %get-tuple-element.27), channel_id=1, source_target_pairs={{2,0},{4,2},{6,4},{8,6},{10,8},{12,10},{14,12},{16,14},{18,16},{20... | collective-permute-start | bytes 589832 | tf_op jit(solution)/shard_map/ppermute | solution.py:36
  119.8 9.7 %collective-permute-start.2 = (bf16[128,768]{1,0:T(8,128)(2,1)S(1)}, bf16[128,768]{1,0:T(8,128)(2,1)S(1)}, u32[]{:S(2)}, u32[]{:S(2)}) collective-permute-start(bf16[128,768]{1,0:T(8,128)(2,1)S(1)} %get-tuple-element.27), channel_id=1, source_target_pairs={{0,2},{2,4},{4,6},{6,8},{8,10},{10,12},{12,14},{14,16},{16,18},{18... | collective-permute-start | bytes 589832 | tf_op jit(solution)/shard_map/ppermute | solution.py:34
  122.1 9.1 %copy-start.66 = (bf16[128,128]{0,1:T(8,128)(2,1)}, bf16[128,128]{0,1:T(8,128)(2,1)S(1)}, u32[]{:S(2)}) copy-start(bf16[128,128]{0,1:T(8,128)(2,1)S(1)} %copy.185) | copy-start | bytes 98308
  122.2 9.6 %copy-start.63 = (bf16[128,128]{0,1:T(8,128)(2,1)}, bf16[128,128]{0,1:T(8,128)(2,1)S(1)}, u32[]{:S(2)}) copy-start(bf16[128,128]{0,1:T(8,128)(2,1)S(1)} %copy.188) | copy-start | bytes 98308
  122.3 10.1 %copy-start.60 = (bf16[128,128]{0,1:T(8,128)(2,1)}, bf16[128,128]{0,1:T(8,128)(2,1)S(1)}, u32[]{:S(2)}) copy-start(bf16[128,128]{0,1:T(8,128)(2,1)S(1)} %copy.191) | copy-start | bytes 98308
  122.5 10.7 %copy-start.57 = (bf16[128,128]{0,1:T(8,128)(2,1)}, bf16[128,128]{0,1:T(8,128)(2,1)S(1)}, u32[]{:S(2)}) copy-start(bf16[128,128]{0,1:T(8,128)(2,1)S(1)} %copy.194) | copy-start | bytes 98308
  122.6 11.2 %copy-start.54 = (bf16[128,128]{0,1:T(8,128)(2,1)}, bf16[128,128]{0,1:T(8,128)(2,1)S(1)}, u32[]{:S(2)}) copy-start(bf16[128,128]{0,1:T(8,128)(2,1)S(1)} %copy.197) | copy-start | bytes 98308
  122.7 12.0 %copy-start.52 = (bf16[128,128]{0,1:T(8,128)(2,1)}, bf16[128,128]{0,1:T(8,128)(2,1)S(1)}, u32[]{:S(2)}) copy-start(bf16[128,128]{0,1:T(8,128)(2,1)S(1)} %copy.200) | copy-start | bytes 98308
  123.0 8.4 %copy-start.46 = (bf16[384,128]{0,1:T(8,128)(2,1)}, bf16[384,128]{0,1:T(8,128)(2,1)S(1)}, u32[]{:S(2)}) copy-start(bf16[384,128]{0,1:T(8,128)(2,1)S(1)} %copy.184) | copy-start | bytes 294916
  129.8 164.9 %copy-start.21 = (bf16[384,128]{0,1:T(8,128)(2,1)}, bf16[384,128]{0,1:T(8,128)(2,1)S(1)}, u32[]{:S(2)}) copy-start(bf16[384,128]{0,1:T(8,128)(2,1)S(1)} %copy.186) | copy-start | bytes 294916
  130.0 2.2 copy-start.50
  130.1 166.1 %copy-start.19 = (bf16[384,128]{0,1:T(8,128)(2,1)}, bf16[384,128]{0,1:T(8,128)(2,1)S(1)}, u32[]{:S(2)}) copy-start(bf16[384,128]{0,1:T(8,128)(2,1)S(1)} %copy.189) | copy-start | bytes 294916
  130.2 2.5 copy-start.48
  130.4 2.1 copy-start.16
  130.5 2.9 copy-start.44
  130.6 211.1 %copy-start.14 = (bf16[384,128]{0,1:T(8,128)(2,1)}, bf16[384,128]{0,1:T(8,128)(2,1)S(1)}, u32[]{:S(2)}) copy-start(bf16[384,128]{0,1:T(8,128)(2,1)S(1)} %copy.195) | copy-start | bytes 294916
  130.8 3.6 copy-start.42
  130.9 212.0 %copy-start.12 = (bf16[384,128]{0,1:T(8,128)(2,1)}, bf16[384,128]{0,1:T(8,128)(2,1)S(1)}, u32[]{:S(2)}) copy-start(bf16[384,128]{0,1:T(8,128)(2,1)S(1)} %copy.198) | copy-start | bytes 294916
  131.1 3.9 copy-start.40
  131.2 3.5 copy-start.10
  135.0 56.0 %copy-start.33 = (f32[2,128,384]{2,1,0:T(8,128)}, f32[2,128,384]{2,1,0:T(8,128)S(1)}, u32[]{:S(2)}) copy-start(f32[2,128,384]{2,1,0:T(8,128)S(1)} %fusion.21) | copy-start | bytes 1179652
  191.0 88.5 %copy-start.5 = (f32[128,768]{1,0:T(8,128)}, f32[128,768]{1,0:T(8,128)S(1)}, u32[]{:S(2)}) copy-start(f32[128,768]{1,0:T(8,128)S(1)} %get-tuple-element.40) | copy-start | bytes 1179652
  285.7 22.1 %all-to-all-start = ((bf16[8,2,18432]{2,1,0:T(2,128)(2,1)}), bf16[8,2,18432]{2,1,0:T(2,128)(2,1)S(1)}, u32[]{:S(2)}, u32[]{:S(2)}) async-start(bf16[8,2,18432]{2,1,0:T(2,128)(2,1)} %reshape.405), calls=%async_computation | async-start | bytes 1179648 | tf_op jit(solution)/shard_map/all_to_all | solution.py:212
  321.9 4.6 %copy-start.26 = (bf16[8,16,12,64]{3,0,2,1:T(8,128)(2,1)S(1)}, bf16[8,16,12,64]{3,0,2,1:T(8,128)(2,1)}, u32[]{:S(2)}) copy-start(bf16[8,16,12,64]{3,0,2,1:T(8,128)(2,1)} %fusion.7) | copy-start | bytes 589828
  323.1 13.1 %all-to-all-start.1 = ((bf16[8,16,768]{2,1,0:T(8,128)(2,1)}), bf16[8,16,768]{2,1,0:T(8,128)(2,1)S(1)}, u32[]{:S(2)}, u32[]{:S(2)}) async-start(bf16[8,16,768]{2,1,0:T(8,128)(2,1)} %reshape.352), calls=%async_computation.1 | async-start | bytes 393216 | tf_op jit(solution)/shard_map/all_to_all | solution.py:216
  327.7 12.9 %copy-start.17 = (bf16[384,128]{0,1:T(8,128)(2,1)S(1)}, bf16[384,128]{0,1:T(8,128)(2,1)}, u32[]{:S(2)}) copy-start(bf16[384,128]{0,1:T(8,128)(2,1)} %copy-done.16) | copy-start | bytes 294916
  327.7 12.9 %copy-start.61 = (bf16[128,128]{0,1:T(8,128)(2,1)S(1)}, bf16[128,128]{0,1:T(8,128)(2,1)}, u32[]{:S(2)}) copy-start(bf16[128,128]{0,1:T(8,128)(2,1)} %copy-done.60) | copy-start | bytes 98308
  336.2 5.6 %copy-start.25 = (bf16[8,16,768]{2,1,0:T(8,128)(2,1)}, bf16[8,16,768]{2,1,0:T(8,128)(2,1)S(1)}, u32[]{:S(2)}) copy-start(bf16[8,16,768]{2,1,0:T(8,128)(2,1)S(1)} %all-to-all-done.1) | copy-start | bytes 589828
  336.2 18.2 %all-to-all-start.4 = ((bf16[8,16,2304]{2,1,0:T(8,128)(2,1)}), bf16[8,16,2304]{2,1,0:T(8,128)(2,1)}, u32[]{:S(2)}, u32[]{:S(2)}) async-start(bf16[8,16,2304]{2,1,0:T(8,128)(2,1)} %pad_maximum_fusion.2), calls=%async_computation.4 | async-start | bytes 1179648 | tf_op jit(solution)/shard_map/all_to_all | solution.py:216
  344.0 10.4 %copy-start.3 = (bf16[768,2304]{1,0:T(8,128)(2,1)S(1)}, bf16[768,2304]{1,0:T(8,128)(2,1)}, u32[]{:S(2)}) copy-start(bf16[768,2304]{1,0:T(8,128)(2,1)} %all-gather.8.cloned.1.call-done) | copy-start | bytes 10616836
  354.4 2.7 copy-start.6
  354.4 2.7 copy-start.24
  354.4 2.7 copy-start.81
  359.6 1.5 copy-start.76
  359.6 1.5 copy-start.39
  359.6 1.5 copy-start.49
  360.2 1.4 copy-start.62
  360.5 1.5 copy-start.74
  360.5 1.5 copy-start.38
  360.5 1.5 copy-start.45
  361.1 1.4 copy-start.59
  361.4 1.5 copy-start.72
  361.4 1.5 copy-start.37
  361.4 1.5 copy-start.43
  362.3 1.5 copy-start.36
  362.3 1.4 copy-start.41
  373.1 14.1 %collective-permute-start.5 = (bf16[128,768]{0,1:T(8,128)(2,1)S(1)}, bf16[128,768]{0,1:T(8,128)(2,1)S(1)}, u32[]{:S(2)}, u32[]{:S(2)}) collective-permute-start(bf16[128,768]{0,1:T(8,128)(2,1)S(1)} %get-tuple-element.5), channel_id=1, source_target_pairs={{2,0},{4,2},{6,4},{8,6},{10,8},{12,10},{14,12},{16,14},{18,16},{20... | collective-permute-start | bytes 589832 | tf_op jit(solution)/shard_map/ppermute | solution.py:36
  376.7 10.8 %collective-permute-start.4 = (bf16[128,768]{0,1:T(8,128)(2,1)S(1)}, bf16[128,768]{0,1:T(8,128)(2,1)S(1)}, u32[]{:S(2)}, u32[]{:S(2)}) collective-permute-start(bf16[128,768]{0,1:T(8,128)(2,1)S(1)} %get-tuple-element.4), channel_id=1, source_target_pairs={{0,2},{2,4},{4,6},{6,8},{8,10},{10,12},{12,14},{14,16},{16,18},{18... | collective-permute-start | bytes 589832 | tf_op jit(solution)/shard_map/ppermute | solution.py:34
  379.1 15.9 %copy-start.2 = (bf16[768,2304]{1,0:T(8,128)(2,1)S(1)}, bf16[768,2304]{1,0:T(8,128)(2,1)}, u32[]{:S(2)}) copy-start(bf16[768,2304]{1,0:T(8,128)(2,1)} %all-gather.4.cloned.1.call-done) | copy-start | bytes 10616836
  379.2 15.8 %copy-start.8 = (bf16[1,128,768]{2,1,0:T(8,128)(2,1)S(1)}, bf16[1,128,768]{2,1,0:T(8,128)(2,1)}, u32[]{:S(2)}) copy-start(bf16[1,128,768]{2,1,0:T(8,128)(2,1)} %param.7) | copy-start | bytes 589828
  379.2 9.2 %collective-permute-start.7 = (bf16[128,768]{0,1:T(8,128)(2,1)S(1)}, bf16[128,768]{0,1:T(8,128)(2,1)S(1)}, u32[]{:S(2)}, u32[]{:S(2)}) collective-permute-start(bf16[128,768]{0,1:T(8,128)(2,1)S(1)} %get-tuple-element.3), channel_id=1, source_target_pairs={{2,0},{4,2},{6,4},{8,6},{10,8},{12,10},{14,12},{16,14},{18,16},{20... | collective-permute-start | bytes 589832 | tf_op jit(solution)/shard_map/ppermute | solution.py:36
  385.2 9.7 %collective-permute-start.6 = (bf16[128,768]{0,1:T(8,128)(2,1)S(1)}, bf16[128,768]{0,1:T(8,128)(2,1)S(1)}, u32[]{:S(2)}, u32[]{:S(2)}) collective-permute-start(bf16[128,768]{0,1:T(8,128)(2,1)S(1)} %get-tuple-element.2), channel_id=1, source_target_pairs={{0,2},{2,4},{4,6},{6,8},{8,10},{10,12},{12,14},{14,16},{16,18},{18... | collective-permute-start | bytes 589832 | tf_op jit(solution)/shard_map/ppermute | solution.py:34
  (36 other events, 39.3 us)
Sparse Core Ops, SparseCore 0:
  11.2 93.0 all-gather.3
  107.5 81.6 all-gather.5
  192.4 84.2 all-gather.7
